TPU v7x, 512 devices: a whole 4x8x8 slice. The times are simulated.
512 devices in a mesh: length: 16 (over z, core), girth: 32 (over x, y).
Axes of the slice: x: 4, y: 8, z: 8, core: 2. Of those that a mesh axis runs over, the one named last changes fastest.
Arguments:
- wave_amplitude: bfloat16 [6, 2048, 65536], P(None, 'length', 'girth'), may hold values from -6 to 6
- load_bank: bfloat16 [65536, 256], P('girth'), may hold values from -0.125 to 0.125
- freq_owner: int32 [1], replicated, may hold values from 0 to 31
- thickness_class: int32 [2048, 8192], P('length', 'girth'), may hold values from 0 to 7
- class_stiffness: float32 [8], replicated, may hold values from 0.5 to 4
- coupling: float32 [6, 6], replicated, may hold values from -0.15 to 2, as said below
- stress_map: float32 [4, 6], replicated, may hold values from -2.5 to 2.5
- psd_weight: float32 [1], replicated, may hold values from 0.5 to 2
- hotspot_tile: int32 [16, 1024], P('length', 'girth'), may hold values from 0 to 127
- hotspot_owner: int32 [16, 1024, 1], P('length', 'girth'), may hold values from 0 to 31; in each aligned block of 32 rows (0 to 31, 32 to 63, ..., all dimensions but the last counted through in order) at most 2 rows name the same one
- prior_moments: float32 [16, 32, 32, 2, 2, 256], P('length', 'girth'), may hold values from 0.1 to 1
Outputs:
- response: float32 [6, 2048, 8192], P(None, 'length', 'girth')
- hotspot_moments: float32 [16, 32, 32, 2, 2, 256], P('length', 'girth')
Inputs may be any that keep to these rules, and one draw needn't show every extreme that they name: `hotspot_owner`: in each device's list of 32 hotspots no owner is named more than 2 times, and in some lists an owner is named exactly 2 times. `coupling`: Symmetric; each diagonal entry is at least 1 and exceeds the sum of the magnitudes of the other entries of its row.
All inputs are finite; a program needn't handle non-finite values.
Results may differ from a plain program's by a relative error of at most 0.0003.
Values may be sent and summed in bfloat16 or wider, within the bound.
No kernel may reach another device: no remote copies, remote signals or barrier semaphores. Data moves between devices by JAX's collectives and lax.ppermute only.
A program may use at most 64 MiB of HBM per device.

v0:
```python
import math
import jax
import jax.numpy as jnp
from jax import lax
from jax.sharding import PartitionSpec as P

SWEEPS = 4
CAP = 2


def spread(block, axis, source):
    block = jnp.where(lax.axis_index(axis) == source, block, jnp.zeros_like(block))
    return lax.psum(block, axis)


def padded_2(block, sides, width):
    for axis, dim in sides:
        count = lax.axis_size(axis)
        forward = [(i, i + 1) for i in range(count - 1)]
        backward = [(target, source) for source, target in forward]
        low = lax.ppermute(
            lax.slice_in_dim(block, block.shape[dim] - width, None, axis=dim), axis, forward
        )
        high = lax.ppermute(lax.slice_in_dim(block, 0, width, axis=dim), axis, backward)
        block = jnp.concatenate([low, block, high], axis=dim)
    return block


def chebyshev_weight(sweep):
    return 1.0 / (1.0 + 0.9 * math.cos(math.pi * (2 * sweep + 1) / (2 * SWEEPS)))


def operate_padded(padded, stiffness, coupling):
    centre = padded[:, 1:-1, 1:-1]
    beside = padded[:, 2:, 1:-1] + padded[:, :-2, 1:-1] + padded[:, 1:-1, 2:] + padded[:, 1:-1, :-2]
    mixing = jnp.einsum("ab,bij->aij", coupling, centre, precision=lax.Precision.HIGHEST)
    return stiffness * (4.0 * centre - beside) + mixing


def square_pairs(values, axis_at):
    first = jnp.take(values, 0, axis=axis_at)
    second = jnp.take(values, 1, axis=axis_at)
    third = jnp.take(values, 2, axis=axis_at)
    fourth = jnp.take(values, 3, axis=axis_at)
    return jnp.stack(
        [first * first + second * second, third * third + fourth * fourth], axis=axis_at
    )


def on_device(
    wave_amplitude,
    load_bank,
    freq_owner,
    thickness_class,
    class_stiffness,
    coupling,
    stress_map,
    psd_weight,
    hotspot_tile,
    hotspot_owner,
    prior_moments,
):
    row_count = wave_amplitude.shape[1]
    girth_cells = load_bank.shape[1]
    mode_count = load_bank.shape[0]
    amplitude = wave_amplitude.reshape(6 * row_count, mode_count)
    root = freq_owner[0]
    factors = spread(load_bank, "girth", root)
    loading = jnp.dot(amplitude, factors, preferred_element_type=jnp.float32)
    loading = loading.reshape(6, row_count, girth_cells)
    stiffness = jnp.zeros((row_count, girth_cells), jnp.float32)
    for level in range(class_stiffness.shape[0]):
        stiffness = stiffness + jnp.where(thickness_class == level, class_stiffness[level], 0.0)
    coupling_diag = jnp.diagonal(coupling)[:, None, None]
    diagonal = 4.0 * stiffness[None] + coupling_diag
    motion = chebyshev_weight(0) * (loading / diagonal)
    for sweep in range(1, SWEEPS):
        padded = padded_2(motion, (("length", 1), ("girth", 2)), 1)
        applied = operate_padded(padded, stiffness, coupling)
        motion = motion + chebyshev_weight(sweep) * ((loading - applied) / diagonal)
    girth_count = lax.axis_size("girth")
    tile_ids = hotspot_tile[0]
    owner_ids = hotspot_owner[0, :, 0]
    listed = owner_ids.shape[0]
    positions = jnp.arange(listed, dtype=jnp.int32)
    matching = owner_ids[:, None] == owner_ids[None, :]
    earlier = positions[None, :] < positions[:, None]
    slot_rank = jnp.sum(jnp.logical_and(matching, earlier).astype(jnp.int32), axis=1)
    target = owner_ids * CAP + slot_rank
    stresses = stiffness[:, None, :] * jnp.einsum(
        "ka,aij->ikj", stress_map, motion, precision=lax.Precision.HIGHEST
    )
    stress_rows = jnp.take(stresses, tile_ids, axis=0)
    outbox = jnp.zeros((girth_count * CAP, 4, girth_cells), jnp.float32).at[target].set(stress_rows)
    outbox = outbox.reshape(girth_count, CAP, 4, girth_cells)
    received = lax.all_to_all(outbox, "girth", split_axis=0, concat_axis=0, tiled=True)
    hotspot_moments = prior_moments + (psd_weight[0] * square_pairs(received, 2))[None, None]
    return (motion, hotspot_moments)


def solution(mesh):
    return jax.shard_map(
        on_device,
        mesh=mesh,
        in_specs=(
            P(None, "length", "girth"),
            P("girth", None),
            P(),
            P("length", "girth"),
            P(),
            P(),
            P(),
            P(),
            P("length", "girth"),
            P("length", "girth", None),
            P("length", "girth", None, None, None, None),
        ),
        out_specs=(P(None, "length", "girth"), P("length", "girth", None, None, None, None)),
        check_vma=False,
    )
```

profile of v0, /device:TPU:264, one launch (start us, length us, event | category | flops | bytes accessed | tf_op | source)
XLA Modules:
  0.0 299.6 jit_solution(5316711973554912137)
XLA Ops:
  10.5 5.3 %broadcast_multiply_fusion.1 = (f32[128,256]{1,0:T(8,128)S(1)}, f32[128,256]{1,0:T(8,128)S(1)}) fusion(f32[]{:T(128)} %bitcast.11, s32[128,256]{1,0:T(8,128)S(1)} %copy-done.6, f32[]{:T(128)} %bitcast.10, f32[]{:T(128)} %bitcast.9, f32[]{:T(128)} %bitcast.8, f32[]{:T(128)} %bitcast.7, f32[]{:T(128)} %bitcast.6, f32[]{:T(128)} %bitcast.5, f32[]{:T(128)} %bitcast.4), kind=kLoop, calls=%fused_computation.85 | loop fusion | flops 786432 | bytes 393248 | tf_op jit(solution)/shard_map/mul | solution.py:75
  15.7 156.9 %all-reduce.2.cloned.1.call-done = bf16[2048,256]{1,0:T(8,128)(2,1)} async-done(((bf16[2048,256]{1,0:T(8,128)(2,1)}), bf16[2048,256]{1,0:T(8,128)(2,1)}) %all-reduce.2.cloned.1.call-update) | async-done | bytes 1048592 | tf_op jit(solution)/shard_map/psum | solution.py:13
  172.7 3.1 %convolution_bitcast_fusion.3 = f32[768,256]{0,1:T(8,128)} fusion(bf16[2048,256]{1,0:T(8,128)(2,1)} %all-reduce.2.cloned.1.call-done, bf16[768,2048]{1,0:T(8,128)(2,1)S(1)} %bitcast.120), kind=kOutput, calls=%fused_computation.22 | convolution fusion | flops 805306368 | bytes 4980736 | tf_op jit(solution)/shard_map/dot_general | solution.py:69
  175.8 2.3 copy.53
  179.9 1.9 collective-permute-start
  181.8 2.4 collective-permute-start.1
  184.3 3.8 %collective-permute-done.1 = f32[6,1,256]{2,0,1:T(8,128)S(1)} collective-permute-done((f32[6,1,256]{2,0,1:T(8,128)S(1)}, f32[6,1,256]{2,0,1:T(8,128)S(1)}, u32[]{:S(2)}, u32[]{:S(2)}) %collective-permute-start.1) | collective-permute-done | bytes 6176 | tf_op jit(solution)/shard_map/ppermute | solution.py:21
  190.6 3.4 %collective-permute-start.2 = (f32[6,130,1]{1,2,0:T(1,128)S(1)}, f32[6,130,1]{1,2,0:T(1,128)S(1)}, u32[]{:S(2)}, u32[]{:S(2)}) collective-permute-start(f32[6,130,1]{1,2,0:T(1,128)S(1)} %copy.55), channel_id=1, source_target_pairs={{1,0},{2,1},{3,2},{4,3},{5,4},{6,5},{7,6},{8,7},{9,8},{10,9},{11,1... | collective-permute-start | bytes 9368 | tf_op jit(solution)/shard_map/ppermute | solution.py:24
  195.3 2.4 collective-permute-start.3
  202.0 6.4 %fusion.11 = f32[6,128,256]{2,0,1:T(8,128)S(1)} fusion(f32[6,128,256]{2,0,1:T(8,128)} %copy-done.2, f32[6,128,256]{2,1,0:T(8,128)} %bitcast.122, f32[6,130,1]{2,0,1:T(8,128)} %copy.58, f32[6,1,256]{2,0,1:T(8,128)S(1)} %collective-permute-done, f32[6,1,256]{2,0,1:T(8,128)S(1)} %collective-permute-done.1, f32[6,130,1]{2,0,1:T(8,128)} %copy.56, ...), kind=kOutput, calls=%fused_computation.21 | convolution fusion | flops 18284544 | bytes 2640136 | tf_op jit(solution)/shard_map/ab,bij->aij/dot_general | solution.py:36
  208.4 1.9 collective-permute-start.4
  210.4 2.4 collective-permute-start.5
  212.8 3.7 %collective-permute-done.5 = f32[6,1,256]{2,0,1:T(8,128)S(1)} collective-permute-done((f32[6,1,256]{2,0,1:T(8,128)S(1)}, f32[6,1,256]{2,0,1:T(8,128)S(1)}, u32[]{:S(2)}, u32[]{:S(2)}) %collective-permute-start.5) | collective-permute-done | bytes 6176 | tf_op jit(solution)/shard_map/ppermute | solution.py:21
  219.1 1.9 collective-permute-start.6
  222.4 3.9 %collective-permute-start.7 = (f32[6,130,1]{1,2,0:T(1,128)S(1)}, f32[6,130,1]{1,2,0:T(1,128)S(1)}, u32[]{:S(2)}, u32[]{:S(2)}) collective-permute-start(f32[6,130,1]{1,2,0:T(1,128)S(1)} %copy.62), channel_id=1, source_target_pairs={{0,1},{1,2},{2,3},{3,4},{4,5},{5,6},{6,7},{7,8},{8,9},{9,10},{10,1... | collective-permute-start | bytes 9368 | tf_op jit(solution)/shard_map/ppermute | solution.py:21
  229.1 6.4 %fusion.7 = f32[6,128,256]{2,0,1:T(8,128)S(1)} fusion(f32[6,128,256]{2,0,1:T(8,128)} %copy-done.5, f32[6,128,256]{2,1,0:T(8,128)} %bitcast.123, f32[6,130,1]{2,0,1:T(8,128)} %copy.63, f32[6,1,256]{2,0,1:T(8,128)S(1)} %collective-permute-done.4, f32[6,1,256]{2,0,1:T(8,128)S(1)} %collective-permute-done.5, f32[6,130,1]{2,0,1:T(8,128)} %copy.61, ...), kind=kOutput, calls=%fused_computation.16 | convolution fusion | flops 18087936 | bytes 2640136 | tf_op jit(solution)/shard_map/ab,bij->aij/dot_general | solution.py:36
  237.4 2.4 collective-permute-start.9
  239.9 3.7 %collective-permute-done.9 = f32[6,1,256]{2,0,1:T(8,128)S(1)} collective-permute-done((f32[6,1,256]{2,0,1:T(8,128)S(1)}, f32[6,1,256]{2,0,1:T(8,128)S(1)}, u32[]{:S(2)}, u32[]{:S(2)}) %collective-permute-start.9) | collective-permute-done | bytes 6176 | tf_op jit(solution)/shard_map/ppermute | solution.py:21
  246.2 1.9 collective-permute-start.10
  249.4 4.1 %collective-permute-start.11 = (f32[6,130,1]{1,2,0:T(1,128)S(1)}, f32[6,130,1]{1,2,0:T(1,128)S(1)}, u32[]{:S(2)}, u32[]{:S(2)}) collective-permute-start(f32[6,130,1]{1,2,0:T(1,128)S(1)} %copy.67), channel_id=1, source_target_pairs={{0,1},{1,2},{2,3},{3,4},{4,5},{5,6},{6,7},{7,8},{8,9},{9,10},{10,1... | collective-permute-start | bytes 9368 | tf_op jit(solution)/shard_map/ppermute | solution.py:21
  256.1 6.4 %fusion.3 = f32[6,128,256]{2,0,1:T(8,128)S(1)} fusion(f32[6,128,256]{2,0,1:T(8,128)} %copy-done.4, f32[6,128,256]{2,1,0:T(8,128)} %bitcast.124, f32[6,130,1]{2,0,1:T(8,128)} %copy.68, f32[6,1,256]{2,0,1:T(8,128)S(1)} %collective-permute-done.8, f32[6,1,256]{2,0,1:T(8,128)S(1)} %collective-permute-done.9, f32[6,130,1]{2,0,1:T(8,128)} %copy.66, ...), kind=kOutput, calls=%fused_computation.11 | convolution fusion | flops 18087936 | bytes 2640136 | tf_op jit(solution)/shard_map/ab,bij->aij/dot_general | solution.py:36
  269.5 11.4 %all-to-all-start = ((f32[32,2,4,256]{3,1,2,0:T(2,128)}), f32[32,2,4,256]{3,1,2,0:T(2,128)S(1)}, u32[]{:S(2)}, u32[]{:S(2)}) async-start(f32[32,2,4,256]{3,1,2,0:T(2,128)} %copy.70), calls=%async_computation | async-start | bytes 524288 | tf_op jit(solution)/shard_map/all_to_all | solution.py:96
  281.6 2.4 copy.76
  284.0 7.9 %all-to-all-done = f32[32,2,4,256]{3,1,2,0:T(2,128)S(1)} async-done(((f32[32,2,4,256]{3,1,2,0:T(2,128)}), f32[32,2,4,256]{3,1,2,0:T(2,128)S(1)}, u32[]{:S(2)}, u32[]{:S(2)}) %all-to-all-start) | async-done | bytes 262176 | tf_op jit(solution)/shard_map/all_to_all | solution.py:96
  (77 shorter events, 35.2 us)
Async XLA Ops:
  7.2 165.5 %copy-start = (bf16[6,128,2048]{2,1,0:T(8,128)(2,1)S(1)}, bf16[6,128,2048]{2,1,0:T(8,128)(2,1)}, u32[]{:S(2)}) copy-start(bf16[6,128,2048]{2,1,0:T(8,128)(2,1)} %param.19) | copy-start | bytes 9437188
  7.2 165.5 %all-reduce.2.cloned.1.call-start = ((), (), s32[]{:S(2)}) async-start(), calls=%async_computation.1 | async-start | bytes 2097152 | tf_op jit(solution)/shard_map/psum | solution.py:13
  8.0 1.1 copy-start.1
  9.1 1.4 copy-start.6
  179.9 8.2 %copy-start.2 = (f32[6,128,256]{2,0,1:T(8,128)}, f32[6,128,256]{2,0,1:T(8,128)S(1)}, u32[]{:S(2)}) copy-start(f32[6,128,256]{2,0,1:T(8,128)S(1)} %broadcast_multiply_fusion) | copy-start | bytes 2359300
  179.9 4.3 %collective-permute-start = (f32[6,1,256]{2,0,1:T(8,128)S(1)}, f32[6,1,256]{2,0,1:T(8,128)S(1)}, u32[]{:S(2)}, u32[]{:S(2)}) collective-permute-start(f32[6,1,256]{2,0,1:T(8,128)S(1)} %get-tuple-element.71), channel_id=1, source_target_pairs={{32,0},{64,32},{96,64},{128,96},{160,128},{192,160},{224,192},{256... | collective-permute-start | bytes 18440 | tf_op jit(solution)/shard_map/ppermute | solution.py:24
  181.8 6.2 %collective-permute-start.1 = (f32[6,1,256]{2,0,1:T(8,128)S(1)}, f32[6,1,256]{2,0,1:T(8,128)S(1)}, u32[]{:S(2)}, u32[]{:S(2)}) collective-permute-start(f32[6,1,256]{2,0,1:T(8,128)S(1)} %get-tuple-element.70), channel_id=1, source_target_pairs={{0,32},{32,64},{64,96},{96,128},{128,160},{160,192},{192,224},{224... | collective-permute-start | bytes 18440 | tf_op jit(solution)/shard_map/ppermute | solution.py:21
  189.3 8.5 %copy-start.10 = (s32[1,32,1]{1,2,0:T(1,128)S(1)}, s32[1,32,1]{1,2,0:T(1,128)}, u32[]{:S(2)}) copy-start(s32[1,32,1]{1,2,0:T(1,128)} %param.28) | copy-start | bytes 388
  190.6 7.4 %collective-permute-start.2 = (f32[6,130,1]{1,2,0:T(1,128)S(1)}, f32[6,130,1]{1,2,0:T(1,128)S(1)}, u32[]{:S(2)}, u32[]{:S(2)}) collective-permute-start(f32[6,130,1]{1,2,0:T(1,128)S(1)} %copy.55), channel_id=1, source_target_pairs={{1,0},{2,1},{3,2},{4,3},{5,4},{6,5},{7,6},{8,7},{9,8},{10,9},{11,1... | collective-permute-start | bytes 9368 | tf_op jit(solution)/shard_map/ppermute | solution.py:24
  195.3 5.5 %collective-permute-start.3 = (f32[6,130,1]{1,2,0:T(1,128)S(1)}, f32[6,130,1]{1,2,0:T(1,128)S(1)}, u32[]{:S(2)}, u32[]{:S(2)}) collective-permute-start(f32[6,130,1]{1,2,0:T(1,128)S(1)} %copy.57), channel_id=1, source_target_pairs={{0,1},{1,2},{2,3},{3,4},{4,5},{5,6},{6,7},{7,8},{8,9},{9,10},{10,1... | collective-permute-start | bytes 9368 | tf_op jit(solution)/shard_map/ppermute | solution.py:21
  208.4 8.2 %copy-start.5 = (f32[6,128,256]{2,0,1:T(8,128)}, f32[6,128,256]{2,0,1:T(8,128)S(1)}, u32[]{:S(2)}) copy-start(f32[6,128,256]{2,0,1:T(8,128)S(1)} %fusion.11) | copy-start | bytes 2359300
  208.4 4.4 %collective-permute-start.4 = (f32[6,1,256]{2,0,1:T(8,128)S(1)}, f32[6,1,256]{2,0,1:T(8,128)S(1)}, u32[]{:S(2)}, u32[]{:S(2)}) collective-permute-start(f32[6,1,256]{2,0,1:T(8,128)S(1)} %get-tuple-element.69), channel_id=1, source_target_pairs={{32,0},{64,32},{96,64},{128,96},{160,128},{192,160},{224,192},{256... | collective-permute-start | bytes 18440 | tf_op jit(solution)/shard_map/ppermute | solution.py:24
  210.4 6.2 %collective-permute-start.5 = (f32[6,1,256]{2,0,1:T(8,128)S(1)}, f32[6,1,256]{2,0,1:T(8,128)S(1)}, u32[]{:S(2)}, u32[]{:S(2)}) collective-permute-start(f32[6,1,256]{2,0,1:T(8,128)S(1)} %get-tuple-element.68), channel_id=1, source_target_pairs={{0,32},{32,64},{64,96},{96,128},{128,160},{160,192},{192,224},{224... | collective-permute-start | bytes 18440 | tf_op jit(solution)/shard_map/ppermute | solution.py:21
  217.8 8.5 %copy-start.11 = (s32[1,32]{1,0:T(1,128)S(1)}, s32[1,32]{1,0:T(1,128)}, u32[]{:S(2)}) copy-start(s32[1,32]{1,0:T(1,128)} %param.27) | copy-start | bytes 388
  219.1 7.2 %collective-permute-start.6 = (f32[6,130,1]{1,2,0:T(1,128)S(1)}, f32[6,130,1]{1,2,0:T(1,128)S(1)}, u32[]{:S(2)}, u32[]{:S(2)}) collective-permute-start(f32[6,130,1]{1,2,0:T(1,128)S(1)} %copy.60), channel_id=1, source_target_pairs={{1,0},{2,1},{3,2},{4,3},{5,4},{6,5},{7,6},{8,7},{9,8},{10,9},{11,1... | collective-permute-start | bytes 9368 | tf_op jit(solution)/shard_map/ppermute | solution.py:24
  222.4 5.5 %collective-permute-start.7 = (f32[6,130,1]{1,2,0:T(1,128)S(1)}, f32[6,130,1]{1,2,0:T(1,128)S(1)}, u32[]{:S(2)}, u32[]{:S(2)}) collective-permute-start(f32[6,130,1]{1,2,0:T(1,128)S(1)} %copy.62), channel_id=1, source_target_pairs={{0,1},{1,2},{2,3},{3,4},{4,5},{5,6},{6,7},{7,8},{8,9},{9,10},{10,1... | collective-permute-start | bytes 9368 | tf_op jit(solution)/shard_map/ppermute | solution.py:21
  235.5 8.2 %copy-start.4 = (f32[6,128,256]{2,0,1:T(8,128)}, f32[6,128,256]{2,0,1:T(8,128)S(1)}, u32[]{:S(2)}) copy-start(f32[6,128,256]{2,0,1:T(8,128)S(1)} %fusion.7) | copy-start | bytes 2359300
  235.5 4.4 %collective-permute-start.8 = (f32[6,1,256]{2,0,1:T(8,128)S(1)}, f32[6,1,256]{2,0,1:T(8,128)S(1)}, u32[]{:S(2)}, u32[]{:S(2)}) collective-permute-start(f32[6,1,256]{2,0,1:T(8,128)S(1)} %get-tuple-element.67), channel_id=1, source_target_pairs={{32,0},{64,32},{96,64},{128,96},{160,128},{192,160},{224,192},{256... | collective-permute-start | bytes 18440 | tf_op jit(solution)/shard_map/ppermute | solution.py:24
  237.4 6.2 %collective-permute-start.9 = (f32[6,1,256]{2,0,1:T(8,128)S(1)}, f32[6,1,256]{2,0,1:T(8,128)S(1)}, u32[]{:S(2)}, u32[]{:S(2)}) collective-permute-start(f32[6,1,256]{2,0,1:T(8,128)S(1)} %get-tuple-element.66), channel_id=1, source_target_pairs={{0,32},{32,64},{64,96},{96,128},{128,160},{160,192},{192,224},{224... | collective-permute-start | bytes 18440 | tf_op jit(solution)/shard_map/ppermute | solution.py:21
  246.2 7.4 %collective-permute-start.10 = (f32[6,130,1]{1,2,0:T(1,128)S(1)}, f32[6,130,1]{1,2,0:T(1,128)S(1)}, u32[]{:S(2)}, u32[]{:S(2)}) collective-permute-start(f32[6,130,1]{1,2,0:T(1,128)S(1)} %copy.65), channel_id=1, source_target_pairs={{1,0},{2,1},{3,2},{4,3},{5,4},{6,5},{7,6},{8,7},{9,8},{10,9},{11,1... | collective-permute-start | bytes 9368 | tf_op jit(solution)/shard_map/ppermute | solution.py:24
  249.4 5.5 %collective-permute-start.11 = (f32[6,130,1]{1,2,0:T(1,128)S(1)}, f32[6,130,1]{1,2,0:T(1,128)S(1)}, u32[]{:S(2)}, u32[]{:S(2)}) collective-permute-start(f32[6,130,1]{1,2,0:T(1,128)S(1)} %copy.67), channel_id=1, source_target_pairs={{0,1},{1,2},{2,3},{3,4},{4,5},{5,6},{6,7},{7,8},{8,9},{9,10},{10,1... | collective-permute-start | bytes 9368 | tf_op jit(solution)/shard_map/ppermute | solution.py:21
  256.1 7.4 %copy-start.9 = (f32[4,6]{1,0:T(4,128)S(1)}, f32[4,6]{1,0:T(4,128)}, u32[]{:S(2)}) copy-start(f32[4,6]{1,0:T(4,128)} %param.25) | copy-start | bytes 292
  269.5 22.4 %all-to-all-start = ((f32[32,2,4,256]{3,1,2,0:T(2,128)}), f32[32,2,4,256]{3,1,2,0:T(2,128)S(1)}, u32[]{:S(2)}, u32[]{:S(2)}) async-start(f32[32,2,4,256]{3,1,2,0:T(2,128)} %copy.70), calls=%async_computation | async-start | bytes 524288 | tf_op jit(solution)/shard_map/all_to_all | solution.py:96
  281.5 10.4 %copy-start.7 = (f32[1,1,32,2,2,256]{5,4,3,2,1,0:T(2,128)S(1)}, f32[1,1,32,2,2,256]{5,4,3,2,1,0:T(2,128)}, u32[]{:S(2)}) copy-start(f32[1,1,32,2,2,256]{5,4,3,2,1,0:T(2,128)} %param.29) | copy-start | bytes 393220
  (2 other events, 1.7 us)
Sparse Core Ops, SparseCore 0:
  11.5 161.1 all-reduce.1
where the time goes:
time: 301 us; the launch traced here: 300 us
  waiting for transfers between devices  178 us (59%)
  starting transfers between devices  42.1 us (14%)
  local copies, waits for them, and re-layouts  30.3 us (10%)
  matrix products  24.2 us (8%)
  between operations  15.9 us (5%)
  other arithmetic  8.78 us (3%)
    psum x1, waiting for transfers between devices, spread(): return lax.psum(block, axis)  157 us
    dot_general x3, matrix products, operate_padded(): jnp.einsum('ab,bij->aij', coupling, centre, precision=lax.Precision.HIGHEST)  19.2 us
    ppermute x6, starting transfers between devices, padded_2(): lax.ppermute(lax.slice_in_dim(block, block.shape[dim] - width, None, axis...  17.7 us
    ppermute x6, waiting for transfers between devices, padded_2(): lax.ppermute(lax.slice_in_dim(block, block.shape[dim] - width, None, axis...  13.5 us
    ppermute x6, starting transfers between devices, padded_2(): lax.ppermute(lax.slice_in_dim(block, 0, width, axis=dim), axis, backward)  13 us
    all_to_all x1, starting transfers between devices, on_device(): lax.all_to_all(outbox, 'girth', split_axis=0, concat_axis=0, tiled=True)  11.4 us
    all_to_all x1, waiting for transfers between devices, on_device(): lax.all_to_all(outbox, 'girth', split_axis=0, concat_axis=0, tiled=True)  7.93 us
    slice x6, local copies, waits for them, and re-layouts, padded_2(): lax.slice_in_dim(block, 0, width, axis=dim)  7.41 us
  transfers between devices with their start and end apart: 14, of which 8 were waited for; matrix products, arithmetic and copies ran while one was open for 6% of the time, Pallas kernels for 0%

commit v1 on v0

--- a/solution.py
+++ b/solution.py
@@ -10,7 +10,7 @@
 
 def spread(block, axis, source):
     block = jnp.where(lax.axis_index(axis) == source, block, jnp.zeros_like(block))
-    return lax.psum(block, axis)
+    return jnp.sum(lax.all_gather(block, axis), axis=0)
 
 
 def padded_2(block, sides, width):

time: 301 us -> 391 us (1.30)
  waiting for transfers between devices: 178 us -> 260 us
  other arithmetic: 8.78 us -> 21.1 us
    all_gather x0 -> x1, waiting for transfers between devices: none -> 234 us  [spread(): return jnp.sum(lax.all_gather(block, axis), axis=0)]
    psum x1 -> x0, waiting for transfers between devices: 157 us -> none  [spread(): return lax.psum(block, axis)]
    reduce_sum x0 -> x1, other arithmetic: none -> 12.4 us  [spread(): return jnp.sum(lax.all_gather(block, axis), axis=0)]
    ppermute x6, waiting for transfers between devices: 0.02 us -> 6.79 us  [padded_2(): lax.ppermute(lax.slice_in_dim(block, 0, width, axis=dim), axis, backward)]
  transfers between devices with their start and end apart: 14 -> 14, of which waited for: 8 -> 8; matrix products, arithmetic and copies ran while one was open for 6% -> 4% of each run, Pallas kernels for 0% -> 0%
where the time goes in v1:
time: 391 us; the launch traced here: 390 us
  waiting for transfers between devices  260 us (66%)
  starting transfers between devices  38.8 us (10%)
  local copies, waits for them, and re-layouts  30.3 us (8%)
  matrix products  24.1 us (6%)
  other arithmetic  21.1 us (5%)
  between operations  15.9 us (4%)
    all_gather x1, waiting for transfers between devices, spread(): return jnp.sum(lax.all_gather(block, axis), axis=0)  234 us
    dot_general x3, matrix products, operate_padded(): jnp.einsum('ab,bij->aij', coupling, centre, precision=lax.Precision.HIGHEST)  19.1 us
    ppermute x6, starting transfers between devices, padded_2(): lax.ppermute(lax.slice_in_dim(block, block.shape[dim] - width, None, axis...  18.2 us
    ppermute x6, starting transfers between devices, padded_2(): lax.ppermute(lax.slice_in_dim(block, 0, width, axis=dim), axis, backward)  12.4 us
    reduce_sum x1, other arithmetic, spread(): return jnp.sum(lax.all_gather(block, axis), axis=0)  12.4 us
    ppermute x6, waiting for transfers between devices, padded_2(): lax.ppermute(lax.slice_in_dim(block, block.shape[dim] - width, None, axis...  11.2 us
    all_to_all x1, starting transfers between devices, on_device(): lax.all_to_all(outbox, 'girth', split_axis=0, concat_axis=0, tiled=True)  8.12 us
    all_to_all x1, waiting for transfers between devices, on_device(): lax.all_to_all(outbox, 'girth', split_axis=0, concat_axis=0, tiled=True)  7.93 us
  transfers between devices with their start and end apart: 14, of which 8 were waited for; matrix products, arithmetic and copies ran while one was open for 4% of the time, Pallas kernels for 0%

profile of v1, /device:TPU:264, one launch (start us, length us, event | category | flops | bytes accessed | tf_op | source)
XLA Modules:
  0.0 390.4 jit_solution(4093551645259123139)
XLA Ops:
  10.5 5.2 %broadcast_multiply_fusion.1 = (f32[128,256]{1,0:T(8,128)S(1)}, f32[128,256]{1,0:T(8,128)S(1)}) fusion(f32[]{:T(128)} %bitcast.12, s32[128,256]{1,0:T(8,128)S(1)} %copy-done.6, f32[]{:T(128)} %bitcast.11, f32[]{:T(128)} %bitcast.10, f32[]{:T(128)} %bitcast.9, f32[]{:T(128)} %bitcast.8, f32[]{:T(128)} %bitcast.7, f32[]{:T(128)} %bitcast.6, f32[]{:T(128)} %bitcast.5), kind=kLoop, calls=%fused_computation.85 | loop fusion | flops 786432 | bytes 393248 | tf_op jit(solution)/shard_map/mul | solution.py:75
  15.7 234.1 %all-gather.3.cloned.1.call-done = bf16[65536,256]{1,0:T(8,128)(2,1)} async-done(((bf16[2048,256]{1,0:T(8,128)(2,1)}), bf16[65536,256]{1,0:T(8,128)(2,1)}) %all-gather.3.cloned.1.call-update) | async-done | bytes 33554448 | tf_op jit(solution)/shard_map/all_gather | solution.py:13
  249.8 12.4 %reduce_sum.23 = bf16[2048,256]{1,0:T(8,128)(2,1)} reduce(bf16[32,2048,256]{2,1,0:T(8,128)(2,1)} %bitcast.122, bf16[]{:T(256)} %constant.104.clone.1), dimensions={0}, to_apply=%region_0.1 | reduce | flops 16252928 | bytes 34603008 | tf_op jit(solution)/shard_map/reduce_sum | solution.py:13
  262.2 3.1 convolution_bitcast_fusion.3
  265.4 2.3 copy.53
  271.4 2.4 collective-permute-start.1
  273.8 3.8 collective-permute-done.1
  280.2 3.4 collective-permute-start.3
  284.9 2.4 collective-permute-start.2
  288.7 2.4 collective-permute-done.2
  292.3 6.3 %fusion.11 = f32[6,128,256]{2,0,1:T(8,128)S(1)} fusion(f32[6,128,256]{2,0,1:T(8,128)} %copy-done.2, f32[6,128,256]{2,1,0:T(8,128)} %bitcast.124, f32[6,130,1]{2,0,1:T(8,128)} %copy.58, f32[6,1,256]{2,0,1:T(8,128)S(1)} %collective-permute-done, f32[6,1,256]{2,0,1:T(8,128)S(1)} %collective-permute-done.1, f32[6,130,1]{2,0,1:T(8,128)} %copy.56, ...), kind=kOutput, calls=%fused_computation.21 | convolution fusion | flops 18284544 | bytes 2640136 | tf_op jit(solution)/shard_map/ab,bij->aij/dot_general | solution.py:36
  300.6 2.4 collective-permute-start.5
  303.0 3.7 collective-permute-done.5
  309.3 3.9 %collective-permute-start.7 = (f32[6,130,1]{1,2,0:T(1,128)S(1)}, f32[6,130,1]{1,2,0:T(1,128)S(1)}, u32[]{:S(2)}, u32[]{:S(2)}) collective-permute-start(f32[6,130,1]{1,2,0:T(1,128)S(1)} %copy.62), channel_id=1, source_target_pairs={{0,1},{1,2},{2,3},{3,4},{4,5},{5,6},{6,7},{7,8},{8,9},{9,10},{10,1... | collective-permute-start | bytes 9368 | tf_op jit(solution)/shard_map/ppermute | solution.py:21
  317.7 2.4 collective-permute-done.6
  321.3 6.4 %fusion.7 = f32[6,128,256]{2,0,1:T(8,128)S(1)} fusion(f32[6,128,256]{2,0,1:T(8,128)} %copy-done.5, f32[6,128,256]{2,1,0:T(8,128)} %bitcast.125, f32[6,130,1]{2,0,1:T(8,128)} %copy.63, f32[6,1,256]{2,0,1:T(8,128)S(1)} %collective-permute-done.4, f32[6,1,256]{2,0,1:T(8,128)S(1)} %collective-permute-done.5, f32[6,130,1]{2,0,1:T(8,128)} %copy.61, ...), kind=kOutput, calls=%fused_computation.16 | convolution fusion | flops 18087936 | bytes 2640136 | tf_op jit(solution)/shard_map/ab,bij->aij/dot_general | solution.py:36
  329.7 2.4 collective-permute-start.9
  332.1 3.7 collective-permute-done.9
  338.4 3.7 collective-permute-start.11
  343.4 2.3 collective-permute-start.10
  350.2 6.4 %fusion.3 = f32[6,128,256]{2,0,1:T(8,128)S(1)} fusion(f32[6,128,256]{2,0,1:T(8,128)} %copy-done.4, f32[6,128,256]{2,1,0:T(8,128)} %bitcast.126, f32[6,130,1]{2,0,1:T(8,128)} %copy.68, f32[6,1,256]{2,0,1:T(8,128)S(1)} %collective-permute-done.8, f32[6,1,256]{2,0,1:T(8,128)S(1)} %collective-permute-done.9, f32[6,130,1]{2,0,1:T(8,128)} %copy.66, ...), kind=kOutput, calls=%fused_computation.11 | convolution fusion | flops 18087936 | bytes 2640136 | tf_op jit(solution)/shard_map/ab,bij->aij/dot_general | solution.py:36
  363.6 8.1 %all-to-all-start = ((f32[32,2,4,256]{3,1,2,0:T(2,128)}), f32[32,2,4,256]{3,1,2,0:T(2,128)S(1)}, u32[]{:S(2)}, u32[]{:S(2)}) async-start(f32[32,2,4,256]{3,1,2,0:T(2,128)} %copy.70), calls=%async_computation | async-start | bytes 524288 | tf_op jit(solution)/shard_map/all_to_all | solution.py:96
  372.3 2.4 copy.76
  374.7 7.9 %all-to-all-done = f32[32,2,4,256]{3,1,2,0:T(2,128)S(1)} async-done(((f32[32,2,4,256]{3,1,2,0:T(2,128)}), f32[32,2,4,256]{3,1,2,0:T(2,128)S(1)}, u32[]{:S(2)}, u32[]{:S(2)}) %all-to-all-start) | async-done | bytes 262176 | tf_op jit(solution)/shard_map/all_to_all | solution.py:96
  (78 shorter events, 40.8 us)
Async XLA Ops:
  7.2 255.1 %copy-start = (bf16[6,128,2048]{2,1,0:T(8,128)(2,1)S(1)}, bf16[6,128,2048]{2,1,0:T(8,128)(2,1)}, u32[]{:S(2)}) copy-start(bf16[6,128,2048]{2,1,0:T(8,128)(2,1)} %param.19) | copy-start | bytes 9437188
  7.2 242.6 %all-gather.3.cloned.1.call-start = ((), (), s32[]{:S(2)}) async-start(), calls=%async_computation.1 | async-start | bytes 34603008 | tf_op jit(solution)/shard_map/all_gather | solution.py:13
  8.0 1.1 copy-start.1
  9.1 1.4 copy-start.6
  269.5 8.2 %copy-start.2 = (f32[6,128,256]{2,0,1:T(8,128)}, f32[6,128,256]{2,0,1:T(8,128)S(1)}, u32[]{:S(2)}) copy-start(f32[6,128,256]{2,0,1:T(8,128)S(1)} %broadcast_multiply_fusion) | copy-start | bytes 2359300
  269.5 4.3 %collective-permute-start = (f32[6,1,256]{2,0,1:T(8,128)S(1)}, f32[6,1,256]{2,0,1:T(8,128)S(1)}, u32[]{:S(2)}, u32[]{:S(2)}) collective-permute-start(f32[6,1,256]{2,0,1:T(8,128)S(1)} %get-tuple-element.71), channel_id=1, source_target_pairs={{32,0},{64,32},{96,64},{128,96},{160,128},{192,160},{224,192},{256... | collective-permute-start | bytes 18440 | tf_op jit(solution)/shard_map/ppermute | solution.py:24
  271.4 6.2 %collective-permute-start.1 = (f32[6,1,256]{2,0,1:T(8,128)S(1)}, f32[6,1,256]{2,0,1:T(8,128)S(1)}, u32[]{:S(2)}, u32[]{:S(2)}) collective-permute-start(f32[6,1,256]{2,0,1:T(8,128)S(1)} %get-tuple-element.70), channel_id=1, source_target_pairs={{0,32},{32,64},{64,96},{96,128},{128,160},{160,192},{192,224},{224... | collective-permute-start | bytes 18440 | tf_op jit(solution)/shard_map/ppermute | solution.py:21
  278.9 8.5 %copy-start.10 = (s32[1,32,1]{1,2,0:T(1,128)S(1)}, s32[1,32,1]{1,2,0:T(1,128)}, u32[]{:S(2)}) copy-start(s32[1,32,1]{1,2,0:T(1,128)} %param.28) | copy-start | bytes 388
  280.2 7.4 %collective-permute-start.3 = (f32[6,130,1]{1,2,0:T(1,128)S(1)}, f32[6,130,1]{1,2,0:T(1,128)S(1)}, u32[]{:S(2)}, u32[]{:S(2)}) collective-permute-start(f32[6,130,1]{1,2,0:T(1,128)S(1)} %copy.57), channel_id=1, source_target_pairs={{0,1},{1,2},{2,3},{3,4},{4,5},{5,6},{6,7},{7,8},{8,9},{9,10},{10,1... | collective-permute-start | bytes 9368 | tf_op jit(solution)/shard_map/ppermute | solution.py:21
  284.9 6.2 %collective-permute-start.2 = (f32[6,130,1]{1,2,0:T(1,128)S(1)}, f32[6,130,1]{1,2,0:T(1,128)S(1)}, u32[]{:S(2)}, u32[]{:S(2)}) collective-permute-start(f32[6,130,1]{1,2,0:T(1,128)S(1)} %copy.55), channel_id=1, source_target_pairs={{1,0},{2,1},{3,2},{4,3},{5,4},{6,5},{7,6},{8,7},{9,8},{10,9},{11,1... | collective-permute-start | bytes 9368 | tf_op jit(solution)/shard_map/ppermute | solution.py:24
  298.6 8.2 %copy-start.5 = (f32[6,128,256]{2,0,1:T(8,128)}, f32[6,128,256]{2,0,1:T(8,128)S(1)}, u32[]{:S(2)}) copy-start(f32[6,128,256]{2,0,1:T(8,128)S(1)} %fusion.11) | copy-start | bytes 2359300
  298.6 4.4 %collective-permute-start.4 = (f32[6,1,256]{2,0,1:T(8,128)S(1)}, f32[6,1,256]{2,0,1:T(8,128)S(1)}, u32[]{:S(2)}, u32[]{:S(2)}) collective-permute-start(f32[6,1,256]{2,0,1:T(8,128)S(1)} %get-tuple-element.69), channel_id=1, source_target_pairs={{32,0},{64,32},{96,64},{128,96},{160,128},{192,160},{224,192},{256... | collective-permute-start | bytes 18440 | tf_op jit(solution)/shard_map/ppermute | solution.py:24
  300.6 6.2 %collective-permute-start.5 = (f32[6,1,256]{2,0,1:T(8,128)S(1)}, f32[6,1,256]{2,0,1:T(8,128)S(1)}, u32[]{:S(2)}, u32[]{:S(2)}) collective-permute-start(f32[6,1,256]{2,0,1:T(8,128)S(1)} %get-tuple-element.68), channel_id=1, source_target_pairs={{0,32},{32,64},{64,96},{96,128},{128,160},{160,192},{192,224},{224... | collective-permute-start | bytes 18440 | tf_op jit(solution)/shard_map/ppermute | solution.py:21
  308.0 8.5 %copy-start.11 = (s32[1,32]{1,0:T(1,128)S(1)}, s32[1,32]{1,0:T(1,128)}, u32[]{:S(2)}) copy-start(s32[1,32]{1,0:T(1,128)} %param.27) | copy-start | bytes 388
  309.3 7.2 %collective-permute-start.7 = (f32[6,130,1]{1,2,0:T(1,128)S(1)}, f32[6,130,1]{1,2,0:T(1,128)S(1)}, u32[]{:S(2)}, u32[]{:S(2)}) collective-permute-start(f32[6,130,1]{1,2,0:T(1,128)S(1)} %copy.62), channel_id=1, source_target_pairs={{0,1},{1,2},{2,3},{3,4},{4,5},{5,6},{6,7},{7,8},{8,9},{9,10},{10,1... | collective-permute-start | bytes 9368 | tf_op jit(solution)/shard_map/ppermute | solution.py:21
  314.6 5.5 %collective-permute-start.6 = (f32[6,130,1]{1,2,0:T(1,128)S(1)}, f32[6,130,1]{1,2,0:T(1,128)S(1)}, u32[]{:S(2)}, u32[]{:S(2)}) collective-permute-start(f32[6,130,1]{1,2,0:T(1,128)S(1)} %copy.60), channel_id=1, source_target_pairs={{1,0},{2,1},{3,2},{4,3},{5,4},{6,5},{7,6},{8,7},{9,8},{10,9},{11,1... | collective-permute-start | bytes 9368 | tf_op jit(solution)/shard_map/ppermute | solution.py:24
  327.7 8.2 %copy-start.4 = (f32[6,128,256]{2,0,1:T(8,128)}, f32[6,128,256]{2,0,1:T(8,128)S(1)}, u32[]{:S(2)}) copy-start(f32[6,128,256]{2,0,1:T(8,128)S(1)} %fusion.7) | copy-start | bytes 2359300
  327.7 4.4 %collective-permute-start.8 = (f32[6,1,256]{2,0,1:T(8,128)S(1)}, f32[6,1,256]{2,0,1:T(8,128)S(1)}, u32[]{:S(2)}, u32[]{:S(2)}) collective-permute-start(f32[6,1,256]{2,0,1:T(8,128)S(1)} %get-tuple-element.67), channel_id=1, source_target_pairs={{32,0},{64,32},{96,64},{128,96},{160,128},{192,160},{224,192},{256... | collective-permute-start | bytes 18440 | tf_op jit(solution)/shard_map/ppermute | solution.py:24
  329.7 6.2 %collective-permute-start.9 = (f32[6,1,256]{2,0,1:T(8,128)S(1)}, f32[6,1,256]{2,0,1:T(8,128)S(1)}, u32[]{:S(2)}, u32[]{:S(2)}) collective-permute-start(f32[6,1,256]{2,0,1:T(8,128)S(1)} %get-tuple-element.66), channel_id=1, source_target_pairs={{0,32},{32,64},{64,96},{96,128},{128,160},{160,192},{192,224},{224... | collective-permute-start | bytes 18440 | tf_op jit(solution)/shard_map/ppermute | solution.py:21
  338.4 7.4 %collective-permute-start.11 = (f32[6,130,1]{1,2,0:T(1,128)S(1)}, f32[6,130,1]{1,2,0:T(1,128)S(1)}, u32[]{:S(2)}, u32[]{:S(2)}) collective-permute-start(f32[6,130,1]{1,2,0:T(1,128)S(1)} %copy.67), channel_id=1, source_target_pairs={{0,1},{1,2},{2,3},{3,4},{4,5},{5,6},{6,7},{7,8},{8,9},{9,10},{10,1... | collective-permute-start | bytes 9368 | tf_op jit(solution)/shard_map/ppermute | solution.py:21
  343.4 5.5 %collective-permute-start.10 = (f32[6,130,1]{1,2,0:T(1,128)S(1)}, f32[6,130,1]{1,2,0:T(1,128)S(1)}, u32[]{:S(2)}, u32[]{:S(2)}) collective-permute-start(f32[6,130,1]{1,2,0:T(1,128)S(1)} %copy.65), channel_id=1, source_target_pairs={{1,0},{2,1},{3,2},{4,3},{5,4},{6,5},{7,6},{8,7},{9,8},{10,9},{11,1... | collective-permute-start | bytes 9368 | tf_op jit(solution)/shard_map/ppermute | solution.py:24
  350.2 7.4 %copy-start.9 = (f32[4,6]{1,0:T(4,128)S(1)}, f32[4,6]{1,0:T(4,128)}, u32[]{:S(2)}) copy-start(f32[4,6]{1,0:T(4,128)} %param.25) | copy-start | bytes 292
  363.6 19.1 %all-to-all-start = ((f32[32,2,4,256]{3,1,2,0:T(2,128)}), f32[32,2,4,256]{3,1,2,0:T(2,128)S(1)}, u32[]{:S(2)}, u32[]{:S(2)}) async-start(f32[32,2,4,256]{3,1,2,0:T(2,128)} %copy.70), calls=%async_computation | async-start | bytes 524288 | tf_op jit(solution)/shard_map/all_to_all | solution.py:96
  372.3 10.4 %copy-start.7 = (f32[1,1,32,2,2,256]{5,4,3,2,1,0:T(2,128)S(1)}, f32[1,1,32,2,2,256]{5,4,3,2,1,0:T(2,128)}, u32[]{:S(2)}) copy-start(f32[1,1,32,2,2,256]{5,4,3,2,1,0:T(2,128)} %param.29) | copy-start | bytes 393220
  (2 other events, 1.7 us)
Sparse Core Ops, SparseCore 0:
  11.2 238.5 all-gather.2
